TPU v7x, 32 devices: a whole 2x2x4 slice. The times are simulated.
32 devices in a mesh: section: 2 (over core), fsdp: 2 (over y), expert: 8 (over z, x).
Axes of the slice: x: 2, y: 2, z: 4, core: 2. Of those that a mesh axis runs over, the one named last changes fastest.
Arguments:
- tokens: bfloat16 [2048, 2048], P(('fsdp', 'expert')), may hold values from -40 to 40
- norm_gain: float32 [2, 2048], P('section'), may hold values from 0.5 to 1.5
- router: bfloat16 [2, 2048, 32], P('section'), may hold values from -0.3125 to 0.3125
- w_gate: bfloat16 [2, 32, 2048, 768], P('section', 'expert', 'fsdp'), may hold values from -0.125 to 0.125
- w_up: bfloat16 [2, 32, 2048, 768], P('section', 'expert', 'fsdp'), may hold values from -0.125 to 0.125
- w_down: bfloat16 [2, 32, 768, 2048], P('section', 'expert', None, 'fsdp'), may hold values from -0.21875 to 0.21875
- routes: int32 [2, 2048, 6], P('section', ('fsdp', 'expert')), may hold values from 0 to 31, all different within a row; in each aligned block of 64 rows (0 to 63, 64 to 127, ..., all dimensions but the last counted through in order) at most 14 rows name the same one
Outputs:
- final_out: bfloat16 [2048, 2048], P(('fsdp', 'expert'), 'section')
- layer_stats: float32 [2], P('section')
Inputs may be any that keep to these rules, and one draw needn't show every extreme that they name: `routes`: each row names 6 different experts; in every aligned block of 64 rows of one layer no expert is named by more than 14 rows, a bound that some block reaches.
All inputs are finite; a program needn't handle non-finite values.
Results may differ from a plain program's by a relative error of at most 0.0065.
Values may be sent and summed in bfloat16 or wider, within the bound.
No kernel may reach another device: no remote copies, remote signals or barrier semaphores. Data moves between devices by JAX's collectives and lax.ppermute only.
A program may use at most 192 MiB of HBM per device.

v0:
```python
import jax
import jax.numpy as jnp
from jax import lax
from jax.sharding import PartitionSpec as P

TOP = 6
BLOCK = 64
epsilon = 1e-06


def other_section(value):
    return lax.ppermute(value, "section", [(0, 1), (1, 0)])


def rms_scaled(hidden_rows, gain_row):
    values = hidden_rows.astype(jnp.float32)
    scale = lax.rsqrt(jnp.mean(values * values, axis=-1, keepdims=True) + epsilon)
    return (values * scale * gain_row).astype(jnp.bfloat16)


def gate_weights(normed, router_weight, route_rows):
    logits = jnp.dot(normed, router_weight, preferred_element_type=jnp.float32)
    scores = jax.nn.sigmoid(logits)
    expert_ids = jnp.arange(router_weight.shape[1], dtype=jnp.int32)
    chosen_mask = (route_rows[:, :, None] == expert_ids[None, None, :]).astype(jnp.float32)
    chosen = jnp.sum(scores[:, None, :] * chosen_mask, axis=2)
    return chosen / jnp.sum(chosen, axis=1, keepdims=True)


def slot_positions(route_rows, experts_count, capacity):
    flat_routes = route_rows.reshape(-1)
    onehot = (flat_routes[:, None] == jnp.arange(experts_count, dtype=jnp.int32)[None, :]).astype(
        jnp.int32
    )
    before = jnp.cumsum(onehot, axis=0) - onehot
    slot_index = jnp.sum(before * onehot, axis=1)
    return (flat_routes * capacity + slot_index).reshape(route_rows.shape)


def expert_layer(entering, route_rows, gain_row, router_weight, weights, capacity):
    gate_w, up_w, down_w = weights
    width = entering.shape[1]
    experts_count = router_weight.shape[1]
    local_experts, chunk, hidden_units = gate_w.shape
    fsdp_count = lax.axis_size("fsdp")
    expert_devices = lax.axis_size("expert")
    peers = fsdp_count * expert_devices
    normed = rms_scaled(entering, gain_row)
    mix_weights = gate_weights(normed, router_weight, route_rows)
    positions = slot_positions(route_rows, experts_count, capacity)
    slot_ids = jnp.arange(experts_count * capacity, dtype=jnp.int32)
    placing = jnp.any(positions[None, :, :] == slot_ids[:, None, None], axis=2).astype(jnp.bfloat16)
    buffer = jnp.dot(placing, normed, preferred_element_type=jnp.float32).astype(jnp.bfloat16)
    outgoing = (
        buffer.reshape(expert_devices, local_experts * capacity, fsdp_count, chunk)
        .transpose(2, 0, 1, 3)
        .reshape(peers, local_experts * capacity, chunk)
    )
    arrived = lax.all_to_all(outgoing, ("fsdp", "expert"), 0, 0, tiled=True)
    arrived = arrived.reshape(peers, local_experts, capacity, chunk)
    gate_part = jnp.einsum("sjcd,jdh->sjch", arrived, gate_w, preferred_element_type=jnp.float32)
    up_part = jnp.einsum("sjcd,jdh->sjch", arrived, up_w, preferred_element_type=jnp.float32)
    both = jnp.concatenate([gate_part, up_part], axis=-1)
    summed = lax.psum_scatter(both, "fsdp", scatter_dimension=0, tiled=True)
    gate_sum = summed[..., :hidden_units]
    up_sum = summed[..., hidden_units:]
    inner_act = (jax.nn.silu(gate_sum) * up_sum).astype(jnp.bfloat16)
    inner_all = lax.all_gather(inner_act, "fsdp", axis=0, tiled=True)
    produced = jnp.einsum(
        "sjch,jhd->sjcd", inner_all, down_w, preferred_element_type=jnp.float32
    ).astype(jnp.bfloat16)
    returned = lax.all_to_all(
        produced.reshape(peers, local_experts * capacity, chunk),
        ("fsdp", "expert"),
        0,
        0,
        tiled=True,
    )
    flat_out = (
        returned.reshape(fsdp_count, expert_devices, local_experts * capacity, chunk)
        .transpose(1, 2, 0, 3)
        .reshape(experts_count * capacity, width)
    )
    picked = jnp.take(flat_out, positions, axis=0)
    branch_sum = jnp.sum(mix_weights[:, :, None] * picked.astype(jnp.float32), axis=1)
    return (entering.astype(jnp.float32) + branch_sum).astype(jnp.bfloat16)


def body(tokens, norm_gain, router, w_gate, w_up, w_down, routes):
    section_index = lax.axis_index("section")
    sections = lax.axis_size("section")
    token_rows, width = tokens.shape
    piece = token_rows // sections
    experts_count = router.shape[2]
    block_capacity = (7 * BLOCK * TOP + 6 * experts_count - 1) // (6 * experts_count)
    capacity = block_capacity * (piece // BLOCK)
    own_weights = (w_gate[0], w_up[0], w_down[0])
    other_weights = tuple((other_section(w) for w in own_weights))
    own_small = (norm_gain[0], router[0], routes[0])
    other_small = tuple((other_section(v) for v in own_small))
    hidden = lax.dynamic_slice_in_dim(tokens, section_index * piece, piece, 0)
    squares = []
    for layer in range(sections):
        mine = section_index == layer
        gain_row, router_weight, route_all = [
            jnp.where(mine, a, b) for a, b in zip(own_small, other_small)
        ]
        weights = tuple((jnp.where(mine, a, b) for a, b in zip(own_weights, other_weights)))
        route_rows = lax.dynamic_slice_in_dim(route_all, section_index * piece, piece, 0)
        hidden = expert_layer(hidden, route_rows, gain_row, router_weight, weights, capacity)
        values = hidden.astype(jnp.float32)
        squares.append(jnp.sum(values * values))
    totals = lax.psum(jnp.stack(squares), ("section", "fsdp", "expert"))
    token_total = token_rows * lax.axis_size("fsdp") * lax.axis_size("expert")
    stats = jnp.sqrt(totals / (token_total * width))
    layer_stats = lax.dynamic_slice_in_dim(stats, section_index, 1, 0)
    half_width = width // 2
    keep = lax.dynamic_slice_in_dim(hidden, section_index * half_width, half_width, 1)
    send = lax.dynamic_slice_in_dim(hidden, (1 - section_index) * half_width, half_width, 1)
    arrived = other_section(send)
    final_out = jnp.where(
        section_index == 0,
        jnp.concatenate([keep, arrived], axis=0),
        jnp.concatenate([arrived, keep], axis=0),
    )
    return (final_out, layer_stats)


def solution(mesh):
    in_specs = (
        P(("fsdp", "expert"), None),
        P("section", None),
        P("section", None, None),
        P("section", "expert", "fsdp", None),
        P("section", "expert", "fsdp", None),
        P("section", "expert", None, "fsdp"),
        P("section", ("fsdp", "expert"), None),
    )
    out_specs = (P(("fsdp", "expert"), "section"), P("section"))
    return jax.shard_map(body, mesh=mesh, in_specs=in_specs, out_specs=out_specs, check_vma=False)
```

profile of v0, /device:TPU:0, one launch (start us, length us, event | category | flops | bytes accessed | tf_op | source)
XLA Modules:
  0.0 542.5 jit_solution(15079160899732492798)
XLA Ops:
  9.0 1.1 fusion.54
  10.1 7.8 %collective-permute-done = s32[128,6]{0,1:T(8,128)S(1)} collective-permute-done((s32[128,6]{0,1:T(8,128)S(1)}, s32[128,6]{0,1:T(8,128)S(1)}, u32[]{:S(2)}, u32[]{:S(2)}) %collective-permute-start) | collective-permute-done | bytes 3104 | tf_op jit(solution)/shard_map/ppermute | solution.py:12
  19.1 0.9 reduce-window.14
  21.4 2.9 convolution_convert_fusion.1
  24.3 4.6 reshape.156
  29.5 52.1 %all_to_all.20 = bf16[16,56,1024]{2,1,0:T(8,128)(2,1)S(1)} all-to-all(bf16[16,56,1024]{2,1,0:T(8,128)(2,1)S(1)} %bitcast.172), channel_id=1, replica_groups=mesh['section'=2,'fsdp'=2,'expert'=8] {'fsdp','expert'}, dimensions={0} | all-to-all | bytes 3670016 | tf_op jit(solution)/shard_map/all_to_all | solution.py:59
  81.5 1.0 copy.67
  82.6 4.6 fusion.27
  87.1 4.6 fusion.30
  91.7 3.1 pad_maximum_fusion
  95.3 2.0 collective-permute-start.3
  97.3 66.4 %reduce-scatter.3.cloned.1.call-done = f32[8,4,14,1536]{3,0,2,1:T(8,128)} async-done(((f32[16,4,14,1536]{3,0,2,1:T(8,128)}), f32[8,4,14,1536]{3,0,2,1:T(8,128)}) %reduce-scatter.3.cloned.1.call-update) | async-done | bytes 2752528 | tf_op jit(solution)/shard_map/reduce_scatter | solution.py:64
  163.7 3.0 fusion.43
  166.8 25.1 %all-gather.3.cloned.1.call-done = bf16[16,4,14,768]{3,0,2,1:T(8,128)(2,1)} async-done(((bf16[8,4,14,768]{3,0,2,1:T(8,128)(2,1)}), bf16[16,4,14,768]{3,0,2,1:T(8,128)(2,1)}) %all-gather.3.cloned.1.call-update) | async-done | bytes 1376272 | tf_op jit(solution)/shard_map/all_gather | solution.py:68
  191.9 4.9 fusion.24
  196.8 2.3 copy.68
  199.1 5.7 %all-to-all-start.1 = ((bf16[16,56,1024]{2,1,0:T(8,128)(2,1)}), bf16[16,56,1024]{2,1,0:T(8,128)(2,1)S(1)}, u32[]{:S(2)}, u32[]{:S(2)}) async-start(bf16[16,56,1024]{2,1,0:T(8,128)(2,1)} %copy.68), calls=%async_computation.2 | async-start | bytes 3670016 | tf_op jit(solution)/shard_map/all_to_all | solution.py:72
  204.9 1.2 collective-permute-start.2
  206.8 0.9 reduce-window.16
  209.0 39.2 %all-to-all-done.1 = bf16[16,56,1024]{2,1,0:T(8,128)(2,1)S(1)} async-done(((bf16[16,56,1024]{2,1,0:T(8,128)(2,1)}), bf16[16,56,1024]{2,1,0:T(8,128)(2,1)S(1)}, u32[]{:S(2)}, u32[]{:S(2)}) %all-to-all-start.1) | async-done | bytes 1835040 | tf_op jit(solution)/shard_map/all_to_all | solution.py:72
  248.2 1.9 copy.69
  250.6 2.5 gather_fusion
  253.1 1.6 reshape.192
  254.7 4.2 multiply_reduce_fusion.1
  258.9 0.8 fusion.52
  260.4 2.3 reshape.163
  262.7 2.0 copy.77
  264.7 49.3 %all_to_all.21 = bf16[16,56,1024]{2,1,0:T(8,128)(2,1)S(1)} all-to-all(bf16[16,56,1024]{2,1,0:T(8,128)(2,1)S(1)} %bitcast.174), channel_id=1, replica_groups=mesh['section'=2,'fsdp'=2,'expert'=8] {'fsdp','expert'}, dimensions={0} | all-to-all | bytes 3670016 | tf_op jit(solution)/shard_map/all_to_all | solution.py:59
  314.0 1.0 copy.78
  315.0 6.4 %fusion.36 = f32[16,4,14,768]{3,0,2,1:T(8,128)S(1)} fusion(bf16[16,4,14,1024]{3,0,2,1:T(8,128)(2,1)S(1)} %bitcast.178, bf16[4,1024,768]{2,1,0:T(8,128)(2,1)} %collective-permute-done.4, pred[]{:T(512)S(6)} %eq.124, bf16[1,4,1024,768]{3,2,1,0:T(8,128)(2,1)} %param.12), kind=kOutput, calls=%fused_computation.36 | convolution fusion | flops 1412431872 | bytes 17170432 | tf_op jit(solution)/shard_map/sjcd,jdh->sjch/dot_general | solution.py:61
  321.4 6.4 %fusion.39 = f32[16,4,14,768]{3,0,2,1:T(8,128)S(1)} fusion(bf16[16,4,14,1024]{3,0,2,1:T(8,128)(2,1)S(1)} %bitcast.179, bf16[4,1024,768]{2,1,0:T(8,128)(2,1)} %collective-permute-done.5, pred[]{:T(512)S(6)} %eq.124, bf16[1,4,1024,768]{3,2,1,0:T(8,128)(2,1)} %param.13), kind=kOutput, calls=%fused_computation.37 | convolution fusion | flops 1412431872 | bytes 17170432 | tf_op jit(solution)/shard_map/sjcd,jdh->sjch/dot_general | solution.py:62
  327.8 3.1 pad_maximum_fusion.1
  331.0 66.3 %reduce-scatter.5.cloned.1.call-done = f32[8,4,14,1536]{3,0,2,1:T(8,128)} async-done(((f32[16,4,14,1536]{3,0,2,1:T(8,128)}), f32[8,4,14,1536]{3,0,2,1:T(8,128)}) %reduce-scatter.5.cloned.1.call-update) | async-done | bytes 2752528 | tf_op jit(solution)/shard_map/reduce_scatter | solution.py:64
  397.3 3.0 fusion.42
  400.3 25.1 %all-gather.5.cloned.1.call-done = bf16[16,4,14,768]{3,0,2,1:T(8,128)(2,1)} async-done(((bf16[8,4,14,768]{3,0,2,1:T(8,128)(2,1)}), bf16[16,4,14,768]{3,0,2,1:T(8,128)(2,1)}) %all-gather.5.cloned.1.call-update) | async-done | bytes 1376272 | tf_op jit(solution)/shard_map/all_gather | solution.py:68
  425.5 6.7 %fusion.33 = bf16[4,1024,16,14]{1,2,3,0:T(8,128)(2,1)S(1)} fusion(bf16[16,4,14,768]{3,0,2,1:T(8,128)(2,1)} %all-gather.5.cloned.1.call-done, bf16[4,768,1024]{2,1,0:T(8,128)(2,1)} %collective-permute-done.3, pred[]{:T(512)S(6)} %eq.124, bf16[1,4,768,1024]{3,2,1,0:T(8,128)(2,1)} %param.14), kind=kOutput, calls=%fused_computation.35 | convolution fusion | flops 1413349376 | bytes 15794177 | tf_op jit(solution)/shard_map/sjch,jhd->sjcd/dot_general | solution.py:69
  432.2 2.3 copy.79
  434.4 6.0 %all-to-all-start.3 = ((bf16[16,56,1024]{2,1,0:T(8,128)(2,1)}), bf16[16,56,1024]{2,1,0:T(8,128)(2,1)S(1)}, u32[]{:S(2)}, u32[]{:S(2)}) async-start(bf16[16,56,1024]{2,1,0:T(8,128)(2,1)} %copy.79), calls=%async_computation.5 | async-start | bytes 3670016 | tf_op jit(solution)/shard_map/all_to_all | solution.py:72
  441.3 40.0 %all-to-all-done.3 = bf16[16,56,1024]{2,1,0:T(8,128)(2,1)S(1)} async-done(((bf16[16,56,1024]{2,1,0:T(8,128)(2,1)}), bf16[16,56,1024]{2,1,0:T(8,128)(2,1)S(1)}, u32[]{:S(2)}, u32[]{:S(2)}) %all-to-all-start.3) | async-done | bytes 1835040 | tf_op jit(solution)/shard_map/all_to_all | solution.py:72
  481.3 1.9 copy.80
  483.7 2.5 gather_fusion.1
  486.2 1.6 reshape.196
  487.8 4.2 multiply_reduce_fusion
  492.0 0.7 multiply_reduce_fusion.2
  492.8 1.4 pad_maximum_fusion.2
  494.1 39.4 %psum.7 = f32[2]{0:T(128)S(1)} all-reduce(f32[2]{0:T(128)S(1)} %pad_maximum_fusion.2), channel_id=1, replica_groups=mesh['section'=2,'fsdp'=2,'expert'=8] {'section','fsdp','expert'}, use_global_device_ids=true, to_apply=%region_20.22 | all-reduce | flops 2 | bytes 16 | tf_op jit(solution)/shard_map/psum | solution.py:113
  534.3 0.7 collective-permute-done.6
  535.0 0.8 maximum_select_fusion
  (87 shorter events, 10.8 us)
Async XLA Ops:
  7.2 156.6 %reduce-scatter.3.cloned.1.call-start = ((), (), s32[]{:S(2)}) async-start(), calls=%async_computation.6 | async-start | bytes 8257536 | tf_op jit(solution)/shard_map/reduce_scatter | solution.py:64
  7.2 75.3 %collective-permute-start.4 = (bf16[4,1024,768]{2,1,0:T(8,128)(2,1)}, bf16[4,1024,768]{2,1,0:T(8,128)(2,1)}, u32[]{:S(2)}, u32[]{:S(2)}) collective-permute-start(bf16[4,1024,768]{2,1,0:T(8,128)(2,1)} %bitcast.187), channel_id=1, source_target_pairs={{0,16},{16,0},{1,17},{17,1},{2,18},{18,2},{3,19},{19,3},{4,20},{20... | collective-permute-start | bytes 18874376 | tf_op jit(solution)/shard_map/ppermute | solution.py:12
  8.5 9.4 %collective-permute-start = (s32[128,6]{0,1:T(8,128)S(1)}, s32[128,6]{0,1:T(8,128)S(1)}, u32[]{:S(2)}, u32[]{:S(2)}) collective-permute-start(s32[128,6]{0,1:T(8,128)S(1)} %bitcast.186), channel_id=1, source_target_pairs={{0,16},{16,0},{1,17},{17,1},{2,18},{18,2},{3,19},{19,3},{4,20},{20... | collective-permute-start | bytes 9224 | tf_op jit(solution)/shard_map/ppermute | solution.py:12
  8.5 12.2 %collective-permute-start.1 = (f32[2048]{0:T(1024)}, f32[2048]{0:T(1024)S(1)}, u32[]{:S(2)}, u32[]{:S(2)}) collective-permute-start(f32[2048]{0:T(1024)} %bitcast.184), channel_id=1, source_target_pairs={{0,16},{16,0},{1,17},{17,1},{2,18},{18,2},{3,19},{19,3},{4,20},{20... | collective-permute-start | bytes 24584 | tf_op jit(solution)/shard_map/ppermute | solution.py:12
  9.0 78.2 %collective-permute-start.5 = (bf16[4,1024,768]{2,1,0:T(8,128)(2,1)}, bf16[4,1024,768]{2,1,0:T(8,128)(2,1)}, u32[]{:S(2)}, u32[]{:S(2)}) collective-permute-start(bf16[4,1024,768]{2,1,0:T(8,128)(2,1)} %bitcast.188), channel_id=1, source_target_pairs={{0,16},{16,0},{1,17},{17,1},{2,18},{18,2},{3,19},{19,3},{4,20},{20... | collective-permute-start | bytes 18874376 | tf_op jit(solution)/shard_map/ppermute | solution.py:12
  94.8 97.1 %all-gather.3.cloned.1.call-start = ((), (), s32[]{:S(2)}) async-start(), calls=%async_computation.7 | async-start | bytes 2064384 | tf_op jit(solution)/shard_map/all_gather | solution.py:68
  95.3 71.4 %collective-permute-start.3 = (bf16[4,768,1024]{2,1,0:T(8,128)(2,1)}, bf16[4,768,1024]{2,1,0:T(8,128)(2,1)}, u32[]{:S(2)}, u32[]{:S(2)}) collective-permute-start(bf16[4,768,1024]{2,1,0:T(8,128)(2,1)} %bitcast.189), channel_id=1, source_target_pairs={{0,16},{16,0},{1,17},{17,1},{2,18},{18,2},{3,19},{19,3},{4,20},{20... | collective-permute-start | bytes 18874376 | tf_op jit(solution)/shard_map/ppermute | solution.py:12
  199.1 5.8 %copy-start.4 = (bf16[1,2048,32]{1,2,0:T(8,128)(2,1)S(1)}, bf16[1,2048,32]{1,2,0:T(8,128)(2,1)}, u32[]{:S(2)}) copy-start(bf16[1,2048,32]{1,2,0:T(8,128)(2,1)} %param.11) | copy-start | bytes 393220
  199.1 9.5 %copy-start.2 = (bf16[128,2048]{1,0:T(8,128)(2,1)S(1)}, bf16[128,2048]{1,0:T(8,128)(2,1)}, u32[]{:S(2)}) copy-start(bf16[128,2048]{1,0:T(8,128)(2,1)} %param.9) | copy-start | bytes 1572868
  199.1 49.1 %all-to-all-start.1 = ((bf16[16,56,1024]{2,1,0:T(8,128)(2,1)}), bf16[16,56,1024]{2,1,0:T(8,128)(2,1)S(1)}, u32[]{:S(2)}, u32[]{:S(2)}) async-start(bf16[16,56,1024]{2,1,0:T(8,128)(2,1)} %copy.68), calls=%async_computation.2 | async-start | bytes 3670016 | tf_op jit(solution)/shard_map/all_to_all | solution.py:72
  204.8 192.5 %reduce-scatter.5.cloned.1.call-start = ((), (), s32[]{:S(2)}) async-start(), calls=%async_computation.8 | async-start | bytes 8257536 | tf_op jit(solution)/shard_map/reduce_scatter | solution.py:64
  204.9 3.7 collective-permute-start.2
  208.6 42.0 %copy-start.6 = (bf16[2048,32]{0,1:T(8,128)(2,1)}, bf16[2048,32]{0,1:T(8,128)(2,1)S(1)}, u32[]{:S(2)}) copy-start(bf16[2048,32]{0,1:T(8,128)(2,1)S(1)} %collective-permute-done.2) | copy-start | bytes 393220
  253.1 5.8 %copy-start.3 = (bf16[128,2048]{1,0:T(8,128)(2,1)S(1)}, bf16[128,2048]{1,0:T(8,128)(2,1)}, u32[]{:S(2)}) copy-start(bf16[128,2048]{1,0:T(8,128)(2,1)} %param.9) | copy-start | bytes 1572868
  259.7 181.1 %copy-start = (bf16[64,2048]{1,0:T(8,128)(2,1)}, bf16[64,2048]{1,0:T(8,128)(2,1)S(1)}, u32[]{:S(2)}) copy-start(bf16[64,2048]{1,0:T(8,128)(2,1)S(1)} %get-tuple-element.13) | copy-start | bytes 786436
  331.0 94.5 %all-gather.5.cloned.1.call-start = ((), (), s32[]{:S(2)}) async-start(), calls=%async_computation.9 | async-start | bytes 2064384 | tf_op jit(solution)/shard_map/all_gather | solution.py:68
  434.4 6.4 %copy-start.5 = (bf16[1,2048,32]{1,2,0:T(8,128)(2,1)S(1)}, bf16[1,2048,32]{1,2,0:T(8,128)(2,1)}, u32[]{:S(2)}) copy-start(bf16[1,2048,32]{1,2,0:T(8,128)(2,1)} %param.11) | copy-start | bytes 393220
  434.4 6.4 %copy-start.7 = (bf16[2048,32]{0,1:T(8,128)(2,1)S(1)}, bf16[2048,32]{0,1:T(8,128)(2,1)}, u32[]{:S(2)}) copy-start(bf16[2048,32]{0,1:T(8,128)(2,1)} %copy-done.6) | copy-start | bytes 393220
  434.4 46.8 %all-to-all-start.3 = ((bf16[16,56,1024]{2,1,0:T(8,128)(2,1)}), bf16[16,56,1024]{2,1,0:T(8,128)(2,1)S(1)}, u32[]{:S(2)}, u32[]{:S(2)}) async-start(bf16[16,56,1024]{2,1,0:T(8,128)(2,1)} %copy.79), calls=%async_computation.5 | async-start | bytes 3670016 | tf_op jit(solution)/shard_map/all_to_all | solution.py:72
  486.1 5.9 %copy-start.1 = (bf16[64,2048]{1,0:T(8,128)(2,1)S(1)}, bf16[64,2048]{1,0:T(8,128)(2,1)}, u32[]{:S(2)}) copy-start(bf16[64,2048]{1,0:T(8,128)(2,1)} %copy-done) | copy-start | bytes 786436
  533.6 1.4 collective-permute-start.6
Sparse Core Ops, SparseCore 0:
  94.9 68.7 reduce-scatter.2
  166.9 24.9 all-gather.2
  331.1 66.1 reduce-scatter.4
  400.5 24.9 all-gather.4
where the time goes:
time: 550 us; the launch traced here: 543 us
  waiting for transfers between devices  271 us (49%)
  blocking collectives  141 us (26%)
  matrix products  37.7 us (7%)
  local copies, waits for them, and re-layouts  32.7 us (6%)
  other arithmetic  29.4 us (5%)
  starting transfers between devices  16.7 us (3%)
  between operations  14.4 us (3%)
    reduce_scatter x2, waiting for transfers between devices, expert_layer(): summed = lax.psum_scatter(both, 'fsdp', scatter_dimension=0, tiled=True)  133 us
    all_to_all x2, blocking collectives, expert_layer(): arrived = lax.all_to_all(outgoing, ('fsdp', 'expert'), 0, 0, tiled=True)  101 us
    all_to_all x2, waiting for transfers between devices, expert_layer(): lax.all_to_all(produced.reshape(peers, local_experts * capacity, chunk),...  79.2 us
    all_gather x2, waiting for transfers between devices, expert_layer(): inner_all = lax.all_gather(inner_act, 'fsdp', axis=0, tiled=True)  50.3 us
    psum x1, blocking collectives, body(): totals = lax.psum(jnp.stack(squares), ('section', 'fsdp', 'expert'))  39.4 us
    all_to_all x2, starting transfers between devices, expert_layer(): lax.all_to_all(produced.reshape(peers, local_experts * capacity, chunk),...  11.7 us
    dot_general x2, matrix products, expert_layer(): jnp.einsum('sjch,jhd->sjcd', inner_all, down_w, preferred_element_type=jn...  11.6 us
  transfers between devices with their start and end apart: 13, of which 8 were waited for; matrix products, arithmetic and copies ran while one was open for 5% of the time, Pallas kernels for 0%

commit v1 on v0

--- a/solution.py
+++ b/solution.py
@@ -6,6 +6,19 @@
 TOP = 6
 BLOCK = 64
 epsilon = 1e-06
+
+
+def pack_the_patch(sheet, axis_k, tile_in):
+    field_out, earlier = (sheet.shape[:axis_k], sheet.shape[axis_k + 1 :])
+    return jnp.moveaxis(sheet.reshape(*field_out, tile_in, -1, *earlier), axis_k, 0)
+
+
+def apply_the_boxes(state, array_axis):
+    state = jnp.moveaxis(state, 0, array_axis)
+    o_now = state.shape
+    return state.reshape(
+        *o_now[:array_axis], o_now[array_axis] * o_now[array_axis + 1], *o_now[array_axis + 2 :]
+    )
 
 
 def other_section(value):
@@ -38,6 +51,19 @@
 
 
 def expert_layer(entering, route_rows, gain_row, router_weight, weights, capacity):
+
+    def bind_edge(shard_in, bus_axis, block_in, field_in):
+        plain, raw_out = (lax.axis_size(bus_axis), lax.axis_index(bus_axis))
+        arr_out = pack_the_patch(shard_in, block_in, plain)
+        nodes = [arr_out[raw_out]]
+        for u in range(1, plain):
+            all_rows = arr_out[(raw_out + u) % plain]
+            nodes.append(
+                lax.ppermute(all_rows, bus_axis, [(num, (num + u) % plain) for num in range(plain)])
+            )
+        arr_out = jnp.stack(nodes, axis=0)[(raw_out - jnp.arange(plain)) % plain]
+        return apply_the_boxes(arr_out, field_in)
+
     gate_w, up_w, down_w = weights
     width = entering.shape[1]
     experts_count = router_weight.shape[1]
@@ -69,12 +95,8 @@
     produced = jnp.einsum(
         "sjch,jhd->sjcd", inner_all, down_w, preferred_element_type=jnp.float32
     ).astype(jnp.bfloat16)
-    returned = lax.all_to_all(
-        produced.reshape(peers, local_experts * capacity, chunk),
-        ("fsdp", "expert"),
-        0,
-        0,
-        tiled=True,
+    returned = bind_edge(
+        produced.reshape(peers, local_experts * capacity, chunk), ("fsdp", "expert"), 0, 0
     )
     flat_out = (
         returned.reshape(fsdp_count, expert_devices, local_experts * capacity, chunk)

time: 550 us -> 567 us (1.031)
  waiting for transfers between devices: 271 us -> 213 us
  starting transfers between devices: 16.7 us -> 67.4 us
  local copies, waits for them, and re-layouts: 32.7 us -> 47.5 us
  blocking collectives: 141 us -> 148 us
    all_to_all x2 -> x0, waiting for transfers between devices: 79.2 us -> none  [expert_layer(): lax.all_to_all(produced.reshape(peers, local_experts * capacity, chunk),...]
    ppermute x0 -> x30, starting transfers between devices: none -> 63.2 us  [bind_edge(): lax.ppermute(all_rows, bus_axis, [(num, (num + u) % plain) for num in ran...]
    ppermute x0 -> x30, waiting for transfers between devices: none -> 25.4 us  [bind_edge(): lax.ppermute(all_rows, bus_axis, [(num, (num + u) % plain) for num in ran...]
    all_to_all x2 -> x0, starting transfers between devices: 11.7 us -> none  [expert_layer(): lax.all_to_all(produced.reshape(peers, local_experts * capacity, chunk),...]
    dynamic_slice x0 -> x2, local copies, waits for them, and re-layouts: none -> 10.8 us  [bind_edge(): all_rows = arr_out[(raw_out + u) % plain]]
    reshape x4 -> x0, local copies, waits for them, and re-layouts: 8.3 us -> none  [the longest x2 4.52 us: expert_layer(): produced.reshape(peers, local_experts * capacity, chunk)]
  transfers between devices with their start and end apart: 13 -> 41, of which waited for: 8 -> 18; matrix products, arithmetic and copies ran while one was open for 5% -> 5% of each run, Pallas kernels for 0% -> 0%
where the time goes in v1:
time: 567 us; the launch traced here: 558 us
  waiting for transfers between devices  213 us (38%)
  blocking collectives  148 us (26%)
  starting transfers between devices  67.4 us (12%)
  local copies, waits for them, and re-layouts  47.5 us (8%)
  matrix products  37.7 us (7%)
  other arithmetic  29.7 us (5%)
  between operations  15.2 us (3%)
    reduce_scatter x2, waiting for transfers between devices, expert_layer(): summed = lax.psum_scatter(both, 'fsdp', scatter_dimension=0, tiled=True)  131 us
    all_to_all x2, blocking collectives, expert_layer(): arrived = lax.all_to_all(outgoing, ('fsdp', 'expert'), 0, 0, tiled=True)  106 us
    ppermute x30, starting transfers between devices, bind_edge(): lax.ppermute(all_rows, bus_axis, [(num, (num + u) % plain) for num in ran...  63.2 us
    all_gather x2, waiting for transfers between devices, expert_layer(): inner_all = lax.all_gather(inner_act, 'fsdp', axis=0, tiled=True)  47.4 us
    psum x1, blocking collectives, body(): totals = lax.psum(jnp.stack(squares), ('section', 'fsdp', 'expert'))  42.1 us
    ppermute x30, waiting for transfers between devices, bind_edge(): lax.ppermute(all_rows, bus_axis, [(num, (num + u) % plain) for num in ran...  25.4 us
    dot_general x2, matrix products, expert_layer(): jnp.einsum('sjch,jhd->sjcd', inner_all, down_w, preferred_element_type=jn...  11.6 us
  transfers between devices with their start and end apart: 41, of which 18 were waited for; matrix products, arithmetic and copies ran while one was open for 5% of the time, Pallas kernels for 0%

profile of v1, /device:TPU:0, one launch (start us, length us, event | category | flops | bytes accessed | tf_op | source)
XLA Modules:
  0.0 558.1 jit_solution(2701070334988508167)
XLA Ops:
  10.1 7.8 %collective-permute-done = s32[128,6]{0,1:T(8,128)S(1)} collective-permute-done((s32[128,6]{0,1:T(8,128)S(1)}, s32[128,6]{0,1:T(8,128)S(1)}, u32[]{:S(2)}, u32[]{:S(2)}) %collective-permute-start) | collective-permute-done | bytes 3104 | tf_op jit(solution)/shard_map/ppermute | solution.py:25
  21.5 2.9 convolution_convert_fusion.1
  24.4 4.6 reshape.193
  29.5 52.1 %all_to_all.10 = bf16[16,56,1024]{2,1,0:T(8,128)(2,1)S(1)} all-to-all(bf16[16,56,1024]{2,1,0:T(8,128)(2,1)S(1)} %bitcast.386), channel_id=1, replica_groups=mesh['section'=2,'fsdp'=2,'expert'=8] {'fsdp','expert'}, dimensions={0} | all-to-all | bytes 3670016 | tf_op jit(solution)/shard_map/all_to_all | solution.py:85
  82.6 4.6 fusion.27
  87.2 4.6 fusion.30
  91.8 3.1 pad_maximum_fusion
  94.9 2.0 collective-permute-start.3
  98.9 64.9 %reduce-scatter.3.cloned.1.call-done = f32[8,4,14,1536]{3,0,2,1:T(8,128)} async-done(((f32[16,4,14,1536]{3,0,2,1:T(8,128)}), f32[8,4,14,1536]{3,0,2,1:T(8,128)}) %reduce-scatter.3.cloned.1.call-update) | async-done | bytes 2752528 | tf_op jit(solution)/shard_map/reduce_scatter | solution.py:90
  163.8 3.0 fusion.43
  168.9 23.1 %all-gather.3.cloned.1.call-done = bf16[16,4,14,768]{3,0,2,1:T(8,128)(2,1)} async-done(((bf16[8,4,14,768]{3,0,2,1:T(8,128)(2,1)}), bf16[16,4,14,768]{3,0,2,1:T(8,128)(2,1)}) %all-gather.3.cloned.1.call-update) | async-done | bytes 1376272 | tf_op jit(solution)/shard_map/all_gather | solution.py:94
  192.0 4.9 fusion.24
  196.9 5.4 constant_dynamic-slice_fusion.19
  205.5 2.4 collective-permute-start.8
  209.5 2.5 collective-permute-start.10
  212.8 2.1 collective-permute-start.11
  216.4 7.8 %collective-permute-done.8 = bf16[1,56,1024]{2,1,0:T(8,128)(2,1)S(1)} collective-permute-done((bf16[1,56,1024]{2,1,0:T(8,128)(2,1)S(1)}, bf16[1,56,1024]{2,1,0:T(8,128)(2,1)S(1)}, u32[]{:S(2)}, u32[]{:S(2)}) %collective-permute-start.8) | collective-permute-done | bytes 114720 | tf_op jit(solution)/shard_map/ppermute | solution.py:62
  228.4 3.1 collective-permute-start.16
  231.5 8.4 %collective-permute-start.17 = (bf16[1,56,1024]{2,1,0:T(8,128)(2,1)S(1)}, bf16[1,56,1024]{2,1,0:T(8,128)(2,1)S(1)}, u32[]{:S(2)}, u32[]{:S(2)}) collective-permute-start(bf16[1,56,1024]{2,1,0:T(8,128)(2,1)S(1)} %bitcast.406), channel_id=1, source_target_pairs={{0,12},{1,13},{2,14},{3,15},{4,0},{5,1},{6,2},{7,3},{8,4},{9,5},{1... | collective-permute-start | bytes 344072 | tf_op jit(solution)/shard_map/ppermute | solution.py:62
  240.0 4.7 collective-permute-start.19
  251.0 2.2 gather_fusion
  253.2 1.9 copy.208
  255.6 2.5 gather_fusion.2
  259.7 4.3 multiply_reduce_fusion.1
  265.5 2.3 reshape.198
  267.7 2.0 copy.216
  269.8 53.9 %all_to_all.11 = bf16[16,56,1024]{2,1,0:T(8,128)(2,1)S(1)} all-to-all(bf16[16,56,1024]{2,1,0:T(8,128)(2,1)S(1)} %bitcast.388), channel_id=1, replica_groups=mesh['section'=2,'fsdp'=2,'expert'=8] {'fsdp','expert'}, dimensions={0} | all-to-all | bytes 3670016 | tf_op jit(solution)/shard_map/all_to_all | solution.py:85
  324.7 6.4 %fusion.36 = f32[16,4,14,768]{3,0,2,1:T(8,128)S(1)} fusion(bf16[16,4,14,1024]{3,0,2,1:T(8,128)(2,1)S(1)} %bitcast.398, bf16[4,1024,768]{2,1,0:T(8,128)(2,1)} %collective-permute-done.4, pred[]{:T(512)S(6)} %eq.158, bf16[1,4,1024,768]{3,2,1,0:T(8,128)(2,1)} %param.12), kind=kOutput, calls=%fused_computation.38 | convolution fusion | flops 1412431872 | bytes 17170432 | tf_op jit(solution)/shard_map/sjcd,jdh->sjch/dot_general | solution.py:87
  331.1 6.4 %fusion.39 = f32[16,4,14,768]{3,0,2,1:T(8,128)S(1)} fusion(bf16[16,4,14,1024]{3,0,2,1:T(8,128)(2,1)S(1)} %bitcast.399, bf16[4,1024,768]{2,1,0:T(8,128)(2,1)} %collective-permute-done.5, pred[]{:T(512)S(6)} %eq.158, bf16[1,4,1024,768]{3,2,1,0:T(8,128)(2,1)} %param.13), kind=kOutput, calls=%fused_computation.39 | convolution fusion | flops 1412431872 | bytes 17170432 | tf_op jit(solution)/shard_map/sjcd,jdh->sjch/dot_general | solution.py:88
  337.5 3.1 pad_maximum_fusion.1
  340.7 66.3 %reduce-scatter.5.cloned.1.call-done = f32[8,4,14,1536]{3,0,2,1:T(8,128)} async-done(((f32[16,4,14,1536]{3,0,2,1:T(8,128)}), f32[8,4,14,1536]{3,0,2,1:T(8,128)}) %reduce-scatter.5.cloned.1.call-update) | async-done | bytes 2752528 | tf_op jit(solution)/shard_map/reduce_scatter | solution.py:90
  407.0 3.0 fusion.42
  410.9 24.3 %all-gather.5.cloned.1.call-done = bf16[16,4,14,768]{3,0,2,1:T(8,128)(2,1)} async-done(((bf16[8,4,14,768]{3,0,2,1:T(8,128)(2,1)}), bf16[16,4,14,768]{3,0,2,1:T(8,128)(2,1)}) %all-gather.5.cloned.1.call-update) | async-done | bytes 1376272 | tf_op jit(solution)/shard_map/all_gather | solution.py:94
  435.2 6.7 %fusion.33 = bf16[4,1024,16,14]{1,2,3,0:T(8,128)(2,1)S(1)} fusion(bf16[16,4,14,768]{3,0,2,1:T(8,128)(2,1)} %all-gather.5.cloned.1.call-done, bf16[4,768,1024]{2,1,0:T(8,128)(2,1)} %collective-permute-done.3, pred[]{:T(512)S(6)} %eq.158, bf16[1,4,768,1024]{3,2,1,0:T(8,128)(2,1)} %param.14), kind=kOutput, calls=%fused_computation.37 | convolution fusion | flops 1413349376 | bytes 15794177 | tf_op jit(solution)/shard_map/sjch,jhd->sjcd/dot_general | solution.py:95
  441.9 5.4 constant_dynamic-slice_fusion.2
  450.5 2.4 collective-permute-start.23
  454.5 2.5 collective-permute-start.25
  457.8 2.1 collective-permute-start.26
  461.4 4.5 collective-permute-done.23
  467.2 4.6 collective-permute-start.30
  471.8 4.6 collective-permute-start.31
  476.4 4.1 collective-permute-start.32
  480.6 2.5 collective-permute-start.33
  484.8 3.0 collective-permute-done.33
  491.7 2.2 gather_fusion.1
  496.3 2.5 gather_fusion.3
  500.3 4.3 multiply_reduce_fusion
  506.7 42.1 %psum.7 = f32[2]{0:T(128)S(1)} all-reduce(f32[2]{0:T(128)S(1)} %pad_maximum_fusion.2), channel_id=1, replica_groups=mesh['section'=2,'fsdp'=2,'expert'=8] {'section','fsdp','expert'}, use_global_device_ids=true, to_apply=%region_20.22 | all-reduce | flops 2 | bytes 16 | tf_op jit(solution)/shard_map/psum | solution.py:135
  (213 shorter events, 57.2 us)
Async XLA Ops:
  7.2 156.6 %reduce-scatter.3.cloned.1.call-start = ((), (), s32[]{:S(2)}) async-start(), calls=%async_computation.4 | async-start | bytes 8257536 | tf_op jit(solution)/shard_map/reduce_scatter | solution.py:90
  7.2 75.4 %collective-permute-start.4 = (bf16[4,1024,768]{2,1,0:T(8,128)(2,1)}, bf16[4,1024,768]{2,1,0:T(8,128)(2,1)}, u32[]{:S(2)}, u32[]{:S(2)}) collective-permute-start(bf16[4,1024,768]{2,1,0:T(8,128)(2,1)} %bitcast.435), channel_id=1, source_target_pairs={{0,16},{16,0},{1,17},{17,1},{2,18},{18,2},{3,19},{19,3},{4,20},{20... | collective-permute-start | bytes 18874376 | tf_op jit(solution)/shard_map/ppermute | solution.py:25
  8.5 9.4 %collective-permute-start = (s32[128,6]{0,1:T(8,128)S(1)}, s32[128,6]{0,1:T(8,128)S(1)}, u32[]{:S(2)}, u32[]{:S(2)}) collective-permute-start(s32[128,6]{0,1:T(8,128)S(1)} %bitcast.434), channel_id=1, source_target_pairs={{0,16},{16,0},{1,17},{17,1},{2,18},{18,2},{3,19},{19,3},{4,20},{20... | collective-permute-start | bytes 9224 | tf_op jit(solution)/shard_map/ppermute | solution.py:25
  8.5 12.3 %collective-permute-start.1 = (f32[2048]{0:T(1024)}, f32[2048]{0:T(1024)S(1)}, u32[]{:S(2)}, u32[]{:S(2)}) collective-permute-start(f32[2048]{0:T(1024)} %bitcast.432), channel_id=1, source_target_pairs={{0,16},{16,0},{1,17},{17,1},{2,18},{18,2},{3,19},{19,3},{4,20},{20... | collective-permute-start | bytes 24584 | tf_op jit(solution)/shard_map/ppermute | solution.py:25
  9.0 78.2 %collective-permute-start.5 = (bf16[4,1024,768]{2,1,0:T(8,128)(2,1)}, bf16[4,1024,768]{2,1,0:T(8,128)(2,1)}, u32[]{:S(2)}, u32[]{:S(2)}) collective-permute-start(bf16[4,1024,768]{2,1,0:T(8,128)(2,1)} %bitcast.436), channel_id=1, source_target_pairs={{0,16},{16,0},{1,17},{17,1},{2,18},{18,2},{3,19},{19,3},{4,20},{20... | collective-permute-start | bytes 18874376 | tf_op jit(solution)/shard_map/ppermute | solution.py:25
  94.9 97.1 %all-gather.3.cloned.1.call-start = ((), (), s32[]{:S(2)}) async-start(), calls=%async_computation.5 | async-start | bytes 2064384 | tf_op jit(solution)/shard_map/all_gather | solution.py:94
  94.9 74.0 %collective-permute-start.3 = (bf16[4,768,1024]{2,1,0:T(8,128)(2,1)}, bf16[4,768,1024]{2,1,0:T(8,128)(2,1)}, u32[]{:S(2)}, u32[]{:S(2)}) collective-permute-start(bf16[4,768,1024]{2,1,0:T(8,128)(2,1)} %bitcast.437), channel_id=1, source_target_pairs={{0,16},{16,0},{1,17},{17,1},{2,18},{18,2},{3,19},{19,3},{4,20},{20... | collective-permute-start | bytes 18874376 | tf_op jit(solution)/shard_map/ppermute | solution.py:25
  96.9 71.5 %collective-permute-start.2 = (bf16[2048,32]{0,1:T(8,128)(2,1)S(1)}, bf16[2048,32]{0,1:T(8,128)(2,1)S(1)}, u32[]{:S(2)}, u32[]{:S(2)}) collective-permute-start(bf16[2048,32]{0,1:T(8,128)(2,1)S(1)} %bitcast.438), channel_id=1, source_target_pairs={{0,16},{16,0},{1,17},{17,1},{2,18},{18,2},{3,19},{19,3},{4,20},{20... | collective-permute-start | bytes 393224 | tf_op jit(solution)/shard_map/ppermute | solution.py:25
  98.9 69.5 %copy-start.4 = (bf16[128,2048]{1,0:T(8,128)(2,1)S(1)}, bf16[128,2048]{1,0:T(8,128)(2,1)}, u32[]{:S(2)}) copy-start(bf16[128,2048]{1,0:T(8,128)(2,1)} %param.9) | copy-start | bytes 1572868
  166.8 240.1 %reduce-scatter.5.cloned.1.call-start = ((), (), s32[]{:S(2)}) async-start(), calls=%async_computation.6 | async-start | bytes 8257536 | tf_op jit(solution)/shard_map/reduce_scatter | solution.py:90
  168.4 28.5 %copy-start.8 = (bf16[2048,32]{0,1:T(8,128)(2,1)}, bf16[2048,32]{0,1:T(8,128)(2,1)S(1)}, u32[]{:S(2)}) copy-start(bf16[2048,32]{0,1:T(8,128)(2,1)S(1)} %collective-permute-done.2) | copy-start | bytes 393220
  202.4 10.4 %collective-permute-start.6 = (bf16[1,56,1024]{2,1,0:T(8,128)(2,1)S(1)}, bf16[1,56,1024]{2,1,0:T(8,128)(2,1)S(1)}, u32[]{:S(2)}, u32[]{:S(2)}) collective-permute-start(bf16[1,56,1024]{2,1,0:T(8,128)(2,1)S(1)} %bitcast.428), channel_id=1, source_target_pairs={{0,1},{1,2},{2,3},{3,4},{4,5},{5,6},{6,7},{7,8},{8,9},{9,10},{10,1... | collective-permute-start | bytes 344072 | tf_op jit(solution)/shard_map/ppermute | solution.py:62
  204.0 10.9 %collective-permute-start.7 = (bf16[1,56,1024]{2,1,0:T(8,128)(2,1)S(1)}, bf16[1,56,1024]{2,1,0:T(8,128)(2,1)S(1)}, u32[]{:S(2)}, u32[]{:S(2)}) collective-permute-start(bf16[1,56,1024]{2,1,0:T(8,128)(2,1)S(1)} %bitcast.426), channel_id=1, source_target_pairs={{0,2},{1,3},{2,4},{3,5},{4,6},{5,7},{6,8},{7,9},{8,10},{9,11},{10,... | collective-permute-start | bytes 344072 | tf_op jit(solution)/shard_map/ppermute | solution.py:62
  205.5 18.7 %collective-permute-start.8 = (bf16[1,56,1024]{2,1,0:T(8,128)(2,1)S(1)}, bf16[1,56,1024]{2,1,0:T(8,128)(2,1)S(1)}, u32[]{:S(2)}, u32[]{:S(2)}) collective-permute-start(bf16[1,56,1024]{2,1,0:T(8,128)(2,1)S(1)} %bitcast.424), channel_id=1, source_target_pairs={{0,3},{1,4},{2,5},{3,6},{4,7},{5,8},{6,9},{7,10},{8,11},{9,12},{10... | collective-permute-start | bytes 344072 | tf_op jit(solution)/shard_map/ppermute | solution.py:62
  208.0 18.4 %collective-permute-start.9 = (bf16[1,56,1024]{2,1,0:T(8,128)(2,1)S(1)}, bf16[1,56,1024]{2,1,0:T(8,128)(2,1)S(1)}, u32[]{:S(2)}, u32[]{:S(2)}) collective-permute-start(bf16[1,56,1024]{2,1,0:T(8,128)(2,1)S(1)} %bitcast.422), channel_id=1, source_target_pairs={{0,4},{1,5},{2,6},{3,7},{4,8},{5,9},{6,10},{7,11},{8,12},{9,13},{1... | collective-permute-start | bytes 344072 | tf_op jit(solution)/shard_map/ppermute | solution.py:62
  209.5 17.5 %collective-permute-start.10 = (bf16[1,56,1024]{2,1,0:T(8,128)(2,1)S(1)}, bf16[1,56,1024]{2,1,0:T(8,128)(2,1)S(1)}, u32[]{:S(2)}, u32[]{:S(2)}) collective-permute-start(bf16[1,56,1024]{2,1,0:T(8,128)(2,1)S(1)} %bitcast.420), channel_id=1, source_target_pairs={{0,5},{1,6},{2,7},{3,8},{4,9},{5,10},{6,11},{7,12},{8,13},{9,14},{... | collective-permute-start | bytes 344072 | tf_op jit(solution)/shard_map/ppermute | solution.py:62
  212.8 15.6 %collective-permute-start.11 = (bf16[1,56,1024]{2,1,0:T(8,128)(2,1)S(1)}, bf16[1,56,1024]{2,1,0:T(8,128)(2,1)S(1)}, u32[]{:S(2)}, u32[]{:S(2)}) collective-permute-start(bf16[1,56,1024]{2,1,0:T(8,128)(2,1)S(1)} %bitcast.418), channel_id=1, source_target_pairs={{0,6},{1,7},{2,8},{3,9},{4,10},{5,11},{6,12},{7,13},{8,14},{9,15},... | collective-permute-start | bytes 344072 | tf_op jit(solution)/shard_map/ppermute | solution.py:62
  214.9 16.6 %collective-permute-start.12 = (bf16[1,56,1024]{2,1,0:T(8,128)(2,1)S(1)}, bf16[1,56,1024]{2,1,0:T(8,128)(2,1)S(1)}, u32[]{:S(2)}, u32[]{:S(2)}) collective-permute-start(bf16[1,56,1024]{2,1,0:T(8,128)(2,1)S(1)} %bitcast.416), channel_id=1, source_target_pairs={{0,7},{1,8},{2,9},{3,10},{4,11},{5,12},{6,13},{7,14},{8,15},{9,0},... | collective-permute-start | bytes 344072 | tf_op jit(solution)/shard_map/ppermute | solution.py:62
  224.3 15.6 %collective-permute-start.13 = (bf16[1,56,1024]{2,1,0:T(8,128)(2,1)S(1)}, bf16[1,56,1024]{2,1,0:T(8,128)(2,1)S(1)}, u32[]{:S(2)}, u32[]{:S(2)}) collective-permute-start(bf16[1,56,1024]{2,1,0:T(8,128)(2,1)S(1)} %bitcast.414), channel_id=1, source_target_pairs={{0,8},{1,9},{2,10},{3,11},{4,12},{5,13},{6,14},{7,15},{8,0},{9,1},... | collective-permute-start | bytes 344072 | tf_op jit(solution)/shard_map/ppermute | solution.py:62
  226.4 13.5 %collective-permute-start.14 = (bf16[1,56,1024]{2,1,0:T(8,128)(2,1)S(1)}, bf16[1,56,1024]{2,1,0:T(8,128)(2,1)S(1)}, u32[]{:S(2)}, u32[]{:S(2)}) collective-permute-start(bf16[1,56,1024]{2,1,0:T(8,128)(2,1)S(1)} %bitcast.412), channel_id=1, source_target_pairs={{0,9},{1,10},{2,11},{3,12},{4,13},{5,14},{6,15},{7,0},{8,1},{9,2},... | collective-permute-start | bytes 344072 | tf_op jit(solution)/shard_map/ppermute | solution.py:62
  227.1 17.6 %collective-permute-start.15 = (bf16[1,56,1024]{2,1,0:T(8,128)(2,1)S(1)}, bf16[1,56,1024]{2,1,0:T(8,128)(2,1)S(1)}, u32[]{:S(2)}, u32[]{:S(2)}) collective-permute-start(bf16[1,56,1024]{2,1,0:T(8,128)(2,1)S(1)} %bitcast.410), channel_id=1, source_target_pairs={{0,10},{1,11},{2,12},{3,13},{4,14},{5,15},{6,0},{7,1},{8,2},{9,3},... | collective-permute-start | bytes 344072 | tf_op jit(solution)/shard_map/ppermute | solution.py:62
  228.4 16.6 %collective-permute-start.16 = (bf16[1,56,1024]{2,1,0:T(8,128)(2,1)S(1)}, bf16[1,56,1024]{2,1,0:T(8,128)(2,1)S(1)}, u32[]{:S(2)}, u32[]{:S(2)}) collective-permute-start(bf16[1,56,1024]{2,1,0:T(8,128)(2,1)S(1)} %bitcast.408), channel_id=1, source_target_pairs={{0,11},{1,12},{2,13},{3,14},{4,15},{5,0},{6,1},{7,2},{8,3},{9,4},{... | collective-permute-start | bytes 344072 | tf_op jit(solution)/shard_map/ppermute | solution.py:62
  231.5 13.5 %collective-permute-start.17 = (bf16[1,56,1024]{2,1,0:T(8,128)(2,1)S(1)}, bf16[1,56,1024]{2,1,0:T(8,128)(2,1)S(1)}, u32[]{:S(2)}, u32[]{:S(2)}) collective-permute-start(bf16[1,56,1024]{2,1,0:T(8,128)(2,1)S(1)} %bitcast.406), channel_id=1, source_target_pairs={{0,12},{1,13},{2,14},{3,15},{4,0},{5,1},{6,2},{7,3},{8,4},{9,5},{1... | collective-permute-start | bytes 344072 | tf_op jit(solution)/shard_map/ppermute | solution.py:62
  239.9 7.0 %collective-permute-start.18 = (bf16[1,56,1024]{2,1,0:T(8,128)(2,1)S(1)}, bf16[1,56,1024]{2,1,0:T(8,128)(2,1)S(1)}, u32[]{:S(2)}, u32[]{:S(2)}) collective-permute-start(bf16[1,56,1024]{2,1,0:T(8,128)(2,1)S(1)} %bitcast.404), channel_id=1, source_target_pairs={{0,13},{1,14},{2,15},{3,0},{4,1},{5,2},{6,3},{7,4},{8,5},{9,6},{10... | collective-permute-start | bytes 344072 | tf_op jit(solution)/shard_map/ppermute | solution.py:62
  240.0 8.7 %collective-permute-start.19 = (bf16[1,56,1024]{2,1,0:T(8,128)(2,1)S(1)}, bf16[1,56,1024]{2,1,0:T(8,128)(2,1)S(1)}, u32[]{:S(2)}, u32[]{:S(2)}) collective-permute-start(bf16[1,56,1024]{2,1,0:T(8,128)(2,1)S(1)} %bitcast.402), channel_id=1, source_target_pairs={{0,14},{1,15},{2,0},{3,1},{4,2},{5,3},{6,4},{7,5},{8,6},{9,7},{10,... | collective-permute-start | bytes 344072 | tf_op jit(solution)/shard_map/ppermute | solution.py:62
  244.7 5.1 collective-permute-start.20
  259.7 4.3 copy-start.5
  264.7 145.6 %copy-start = (bf16[64,2048]{1,0:T(8,128)(2,1)}, bf16[64,2048]{1,0:T(8,128)(2,1)S(1)}, u32[]{:S(2)}) copy-start(bf16[64,2048]{1,0:T(8,128)(2,1)S(1)} %get-tuple-element.13) | copy-start | bytes 786436
  340.6 69.8 %copy-start.7 = (bf16[1,2048,32]{1,2,0:T(8,128)(2,1)S(1)}, bf16[1,2048,32]{1,2,0:T(8,128)(2,1)}, u32[]{:S(2)}) copy-start(bf16[1,2048,32]{1,2,0:T(8,128)(2,1)} %param.11) | copy-start | bytes 393220
  340.7 69.8 %copy-start.9 = (bf16[2048,32]{0,1:T(8,128)(2,1)S(1)}, bf16[2048,32]{0,1:T(8,128)(2,1)}, u32[]{:S(2)}) copy-start(bf16[2048,32]{0,1:T(8,128)(2,1)} %copy-done.8) | copy-start | bytes 393220
  340.7 94.5 %all-gather.5.cloned.1.call-start = ((), (), s32[]{:S(2)}) async-start(), calls=%async_computation.7 | async-start | bytes 2064384 | tf_op jit(solution)/shard_map/all_gather | solution.py:94
  447.3 10.4 %collective-permute-start.21 = (bf16[1,56,1024]{2,1,0:T(8,128)(2,1)S(1)}, bf16[1,56,1024]{2,1,0:T(8,128)(2,1)S(1)}, u32[]{:S(2)}, u32[]{:S(2)}) collective-permute-start(bf16[1,56,1024]{2,1,0:T(8,128)(2,1)S(1)} %bitcast.429), channel_id=1, source_target_pairs={{0,1},{1,2},{2,3},{3,4},{4,5},{5,6},{6,7},{7,8},{8,9},{9,10},{10,1... | collective-permute-start | bytes 344072 | tf_op jit(solution)/shard_map/ppermute | solution.py:62
  448.9 10.9 %collective-permute-start.22 = (bf16[1,56,1024]{2,1,0:T(8,128)(2,1)S(1)}, bf16[1,56,1024]{2,1,0:T(8,128)(2,1)S(1)}, u32[]{:S(2)}, u32[]{:S(2)}) collective-permute-start(bf16[1,56,1024]{2,1,0:T(8,128)(2,1)S(1)} %bitcast.427), channel_id=1, source_target_pairs={{0,2},{1,3},{2,4},{3,5},{4,6},{5,7},{6,8},{7,9},{8,10},{9,11},{10,... | collective-permute-start | bytes 344072 | tf_op jit(solution)/shard_map/ppermute | solution.py:62
  450.5 15.4 %collective-permute-start.23 = (bf16[1,56,1024]{2,1,0:T(8,128)(2,1)S(1)}, bf16[1,56,1024]{2,1,0:T(8,128)(2,1)S(1)}, u32[]{:S(2)}, u32[]{:S(2)}) collective-permute-start(bf16[1,56,1024]{2,1,0:T(8,128)(2,1)S(1)} %bitcast.425), channel_id=1, source_target_pairs={{0,3},{1,4},{2,5},{3,6},{4,7},{5,8},{6,9},{7,10},{8,11},{9,12},{10... | collective-permute-start | bytes 344072 | tf_op jit(solution)/shard_map/ppermute | solution.py:62
  453.0 13.6 %collective-permute-start.24 = (bf16[1,56,1024]{2,1,0:T(8,128)(2,1)S(1)}, bf16[1,56,1024]{2,1,0:T(8,128)(2,1)S(1)}, u32[]{:S(2)}, u32[]{:S(2)}) collective-permute-start(bf16[1,56,1024]{2,1,0:T(8,128)(2,1)S(1)} %bitcast.423), channel_id=1, source_target_pairs={{0,4},{1,5},{2,6},{3,7},{4,8},{5,9},{6,10},{7,11},{8,12},{9,13},{1... | collective-permute-start | bytes 344072 | tf_op jit(solution)/shard_map/ppermute | solution.py:62
  454.5 12.7 %collective-permute-start.25 = (bf16[1,56,1024]{2,1,0:T(8,128)(2,1)S(1)}, bf16[1,56,1024]{2,1,0:T(8,128)(2,1)S(1)}, u32[]{:S(2)}, u32[]{:S(2)}) collective-permute-start(bf16[1,56,1024]{2,1,0:T(8,128)(2,1)S(1)} %bitcast.421), channel_id=1, source_target_pairs={{0,5},{1,6},{2,7},{3,8},{4,9},{5,10},{6,11},{7,12},{8,13},{9,14},{... | collective-permute-start | bytes 344072 | tf_op jit(solution)/shard_map/ppermute | solution.py:62
  457.8 14.0 %collective-permute-start.26 = (bf16[1,56,1024]{2,1,0:T(8,128)(2,1)S(1)}, bf16[1,56,1024]{2,1,0:T(8,128)(2,1)S(1)}, u32[]{:S(2)}, u32[]{:S(2)}) collective-permute-start(bf16[1,56,1024]{2,1,0:T(8,128)(2,1)S(1)} %bitcast.419), channel_id=1, source_target_pairs={{0,6},{1,7},{2,8},{3,9},{4,10},{5,11},{6,12},{7,13},{8,14},{9,15},... | collective-permute-start | bytes 344072 | tf_op jit(solution)/shard_map/ppermute | solution.py:62
  459.9 16.6 %collective-permute-start.27 = (bf16[1,56,1024]{2,1,0:T(8,128)(2,1)S(1)}, bf16[1,56,1024]{2,1,0:T(8,128)(2,1)S(1)}, u32[]{:S(2)}, u32[]{:S(2)}) collective-permute-start(bf16[1,56,1024]{2,1,0:T(8,128)(2,1)S(1)} %bitcast.417), channel_id=1, source_target_pairs={{0,7},{1,8},{2,9},{3,10},{4,11},{5,12},{6,13},{7,14},{8,15},{9,0},... | collective-permute-start | bytes 344072 | tf_op jit(solution)/shard_map/ppermute | solution.py:62
  465.9 14.7 %collective-permute-start.28 = (bf16[1,56,1024]{2,1,0:T(8,128)(2,1)S(1)}, bf16[1,56,1024]{2,1,0:T(8,128)(2,1)S(1)}, u32[]{:S(2)}, u32[]{:S(2)}) collective-permute-start(bf16[1,56,1024]{2,1,0:T(8,128)(2,1)S(1)} %bitcast.415), channel_id=1, source_target_pairs={{0,8},{1,9},{2,10},{3,11},{4,12},{5,13},{6,14},{7,15},{8,0},{9,1},... | collective-permute-start | bytes 344072 | tf_op jit(solution)/shard_map/ppermute | solution.py:62
  466.5 16.5 %collective-permute-start.29 = (bf16[1,56,1024]{2,1,0:T(8,128)(2,1)S(1)}, bf16[1,56,1024]{2,1,0:T(8,128)(2,1)S(1)}, u32[]{:S(2)}, u32[]{:S(2)}) collective-permute-start(bf16[1,56,1024]{2,1,0:T(8,128)(2,1)S(1)} %bitcast.413), channel_id=1, source_target_pairs={{0,9},{1,10},{2,11},{3,12},{4,13},{5,14},{6,15},{7,0},{8,1},{9,2},... | collective-permute-start | bytes 344072 | tf_op jit(solution)/shard_map/ppermute | solution.py:62
  467.2 16.9 %collective-permute-start.30 = (bf16[1,56,1024]{2,1,0:T(8,128)(2,1)S(1)}, bf16[1,56,1024]{2,1,0:T(8,128)(2,1)S(1)}, u32[]{:S(2)}, u32[]{:S(2)}) collective-permute-start(bf16[1,56,1024]{2,1,0:T(8,128)(2,1)S(1)} %bitcast.411), channel_id=1, source_target_pairs={{0,10},{1,11},{2,12},{3,13},{4,14},{5,15},{6,0},{7,1},{8,2},{9,3},... | collective-permute-start | bytes 344072 | tf_op jit(solution)/shard_map/ppermute | solution.py:62
  471.8 12.9 %collective-permute-start.31 = (bf16[1,56,1024]{2,1,0:T(8,128)(2,1)S(1)}, bf16[1,56,1024]{2,1,0:T(8,128)(2,1)S(1)}, u32[]{:S(2)}, u32[]{:S(2)}) collective-permute-start(bf16[1,56,1024]{2,1,0:T(8,128)(2,1)S(1)} %bitcast.409), channel_id=1, source_target_pairs={{0,11},{1,12},{2,13},{3,14},{4,15},{5,0},{6,1},{7,2},{8,3},{9,4},{... | collective-permute-start | bytes 344072 | tf_op jit(solution)/shard_map/ppermute | solution.py:62
  476.4 8.3 %collective-permute-start.32 = (bf16[1,56,1024]{2,1,0:T(8,128)(2,1)S(1)}, bf16[1,56,1024]{2,1,0:T(8,128)(2,1)S(1)}, u32[]{:S(2)}, u32[]{:S(2)}) collective-permute-start(bf16[1,56,1024]{2,1,0:T(8,128)(2,1)S(1)} %bitcast.407), channel_id=1, source_target_pairs={{0,12},{1,13},{2,14},{3,15},{4,0},{5,1},{6,2},{7,3},{8,4},{9,5},{1... | collective-permute-start | bytes 344072 | tf_op jit(solution)/shard_map/ppermute | solution.py:62
  480.6 7.1 %collective-permute-start.33 = (bf16[1,56,1024]{2,1,0:T(8,128)(2,1)S(1)}, bf16[1,56,1024]{2,1,0:T(8,128)(2,1)S(1)}, u32[]{:S(2)}, u32[]{:S(2)}) collective-permute-start(bf16[1,56,1024]{2,1,0:T(8,128)(2,1)S(1)} %bitcast.405), channel_id=1, source_target_pairs={{0,13},{1,14},{2,15},{3,0},{4,1},{5,2},{6,3},{7,4},{8,5},{9,6},{10... | collective-permute-start | bytes 344072 | tf_op jit(solution)/shard_map/ppermute | solution.py:62
  483.1 6.1 %collective-permute-start.34 = (bf16[1,56,1024]{2,1,0:T(8,128)(2,1)S(1)}, bf16[1,56,1024]{2,1,0:T(8,128)(2,1)S(1)}, u32[]{:S(2)}, u32[]{:S(2)}) collective-permute-start(bf16[1,56,1024]{2,1,0:T(8,128)(2,1)S(1)} %bitcast.403), channel_id=1, source_target_pairs={{0,14},{1,15},{2,0},{3,1},{4,2},{5,3},{6,4},{7,5},{8,6},{9,7},{10,... | collective-permute-start | bytes 344072 | tf_op jit(solution)/shard_map/ppermute | solution.py:62
  484.1 6.3 %collective-permute-start.35 = (bf16[1,56,1024]{2,1,0:T(8,128)(2,1)S(1)}, bf16[1,56,1024]{2,1,0:T(8,128)(2,1)S(1)}, u32[]{:S(2)}, u32[]{:S(2)}) collective-permute-start(bf16[1,56,1024]{2,1,0:T(8,128)(2,1)S(1)} %bitcast.401), channel_id=1, source_target_pairs={{0,15},{1,0},{2,1},{3,2},{4,3},{5,4},{6,5},{7,6},{8,7},{9,8},{10,9... | collective-permute-start | bytes 344072 | tf_op jit(solution)/shard_map/ppermute | solution.py:62
  500.3 4.3 copy-start.1
  548.9 1.4 collective-permute-start.36
  (3 other events, 4.6 us)
Sparse Core Ops, SparseCore 0:
  95.0 68.7 reduce-scatter.2
  167.0 24.9 all-gather.2
  340.8 66.1 reduce-scatter.4
  410.1 24.9 all-gather.4
